TPU v7x, 256 devices: a whole 4x4x8 slice. The times are simulated.
256 devices in a mesh: ctx: 16 (over x_lo, z), fsdp: 4 (over y), head: 4 (over x_hi, core).
Axes of the slice: x: 4 (x_hi: 2, x_lo: 2; x = x_hi * 2 + x_lo), y: 4, z: 8, core: 2. Of those that a mesh axis runs over, the one named last changes fastest.
Arguments:
- queries: bfloat16 [4, 8192, 2048], P('fsdp', 'ctx', 'head'), may hold values from -6 to 6
- keys: bfloat16 [4, 8192, 2048], P('fsdp', 'ctx', 'head'), may hold values from -6 to 6
- values: bfloat16 [4, 8192, 2048], P('fsdp', 'ctx', 'head'), may hold values from -6 to 6
- gate_pre: bfloat16 [4, 8192, 2048], P('fsdp', 'ctx', 'head'), may hold values from -6 to 6
- log_decay: float32 [4, 8192, 16], P('fsdp', 'ctx', 'head'), may hold values from -2 to 0, as said below
- out_grad: bfloat16 [4, 8192, 4096], P('fsdp', 'ctx', 'head'), may hold values from -6 to 6
- out_weight: float32 [4096, 2048], P(('ctx', 'fsdp'), 'head'), may hold values from -0.125 to 0.125
- moment_one: float32 [4096, 2048], P(('ctx', 'fsdp'), 'head'), may hold values from -2 to 2
- moment_two: float32 [4096, 2048], P(('ctx', 'fsdp'), 'head'), may hold values from 0.05 to 1
- group_ids: int32 [128], P(('ctx', 'fsdp')), may hold values from 0 to 2
- step_count: int32 [1], replicated, may hold values from 1 to 40
Outputs:
- query_grad: bfloat16 [4, 8192, 2048], P('fsdp', 'ctx', 'head')
- key_grad: bfloat16 [4, 8192, 2048], P('fsdp', 'ctx', 'head')
- value_grad: bfloat16 [4, 8192, 2048], P('fsdp', 'ctx', 'head')
- new_moment_one: float32 [4096, 2048], P(('ctx', 'fsdp'), 'head')
- new_moment_two: float32 [4096, 2048], P(('ctx', 'fsdp'), 'head')
- weight_step: float32 [4096, 2048], P(('ctx', 'fsdp'), 'head')
Inputs may be any that keep to these rules, and one draw needn't show every extreme that they name: `log_decay`: Log-decays per token and head, never positive. `group_ids`: 0 for a frozen block of rows, 1 for one updated without weight decay, 2 for one updated with it.
All inputs are finite; a program needn't handle non-finite values.
Results may differ from a plain program's by a relative error of at most 0.017.
Values may be sent and summed in bfloat16 or wider, within the bound.
No kernel may reach another device: no remote copies, remote signals or barrier semaphores. Data moves between devices by JAX's collectives and lax.ppermute only.
A program may use at most 128 MiB of HBM per device.

v0:
```python
import jax
import jax.numpy as jnp
from jax import lax
from jax.sharding import PartitionSpec as P

HEAD_DIM = 128
SPAN = 256
ROW_BLOCK = 32
NORM_EPS = 1e-06
BETA_ONE = 0.9
BETA_TWO = 0.95
ADAM_EPS = 1e-08
WEIGHT_DECAY = 0.1


def window_scan(gain, state, axis, sign):
    count = lax.axis_size(axis)
    place = lax.axis_index(axis)

    def join(near, far):
        return (near[0] * far[0], near[1] + near[0][:, None, None] * far[1])

    def fetch(value, step):
        pairs = [(i, i + sign * step) for i in range(count) if 0 <= i + sign * step < count]
        got = lax.ppermute(value, axis, pairs)
        source = place - sign * step
        present = (source >= 0) & (source < count)
        return jax.tree.map(lambda g, e: jnp.where(present, g, e), got, identity)

    own = (gain, state)
    identity = (jnp.ones_like(gain), jnp.zeros_like(state))
    near = [fetch(own, step) for step in (1, 2, 3)]
    inner = join(join(near[0], near[1]), near[2])
    window = join(own, inner)
    total = inner
    for step in (4, 8, 12):
        total = join(total, fetch(window, step))
    return total[1]


def decay_mask(cumul):
    along = jnp.swapaxes(cumul, 1, 2)
    spread = along[:, :, :, None] - along[:, :, None, :]
    length = cumul.shape[1]
    lower = jnp.tril(jnp.ones((length, length), jnp.float32))
    return jnp.exp(jnp.minimum(spread, 0.0)) * lower


def per_device(
    queries,
    keys,
    values,
    gate_pre,
    log_decay,
    out_grad,
    out_weight,
    moment_one,
    moment_two,
    group_ids,
    step_count,
):
    tok_local = queries.shape[1]
    head_local = log_decay.shape[2]
    width_local = queries.shape[2]
    blocks = tok_local // SPAN
    shaped = (blocks, SPAN, head_local, HEAD_DIM)
    query_c = queries.reshape(shaped)
    key_c = keys.reshape(shaped)
    value_c = values.reshape(shaped)
    cumul = jnp.cumsum(log_decay.reshape(blocks, SPAN, head_local), axis=1)
    totals = cumul[:, -1, :]
    masking = decay_mask(cumul)
    decay_in = jnp.exp(cumul)[..., None]
    decay_out = jnp.exp(totals[:, None, :] - cumul)[..., None]
    scores = jnp.einsum("cthe,cuhe->chtu", query_c, key_c, preferred_element_type=jnp.float32)
    probs = (scores * masking).astype(jnp.bfloat16)
    intra = jnp.einsum("chtu,cuhe->cthe", probs, value_c, preferred_element_type=jnp.float32)
    scaled = (decay_out * key_c).astype(jnp.bfloat16)
    updates = jnp.einsum("cthe,cthf->chef", scaled, value_c, preferred_element_type=jnp.float32)
    running = jnp.zeros((head_local, HEAD_DIM, HEAD_DIM), jnp.float32)
    leading = jnp.zeros((head_local,), jnp.float32)
    start_list = []
    lead_list = []
    for block in range(blocks):
        start_list.append(running)
        lead_list.append(leading)
        running = jnp.exp(totals[block])[:, None, None] * running + updates[block]
        leading = leading + totals[block]
    local_start = jnp.stack(start_list)
    lead_sums = jnp.stack(lead_list)
    incoming = window_scan(jnp.exp(leading), running, "ctx", 1)
    states = local_start + jnp.exp(lead_sums)[:, :, None, None] * incoming[None]
    rounded = states.astype(jnp.bfloat16)
    inter = decay_in * jnp.einsum(
        "cthe,chef->cthf", query_c, rounded, preferred_element_type=jnp.float32
    )
    attn = intra + inter
    square = jnp.mean(attn * attn, axis=-1, keepdims=True)
    inverse = lax.rsqrt(square + NORM_EPS)
    normed = attn * inverse
    silu_gate = jax.nn.silu(gate_pre.reshape(shaped).astype(jnp.float32))
    mixed = (normed * silu_gate).astype(jnp.bfloat16).reshape(tok_local, width_local)
    features = lax.all_gather(out_grad, "head", axis=2, tiled=True)[0]
    weight_b = out_weight.astype(jnp.bfloat16)
    columns = features
    mixed_grad = jnp.dot(
        columns,
        lax.all_gather(
            lax.all_gather(weight_b, "fsdp", axis=0, tiled=True), "ctx", axis=0, tiled=True
        ),
        preferred_element_type=jnp.float32,
    )
    columns = features
    grad_rows = lax.psum_scatter(
        lax.psum_scatter(
            jnp.einsum("td,th->dh", columns, mixed, preferred_element_type=jnp.float32).astype(
                jnp.bfloat16
            ),
            "ctx",
            scatter_dimension=0,
            tiled=True,
        ).astype(jnp.float32),
        "fsdp",
        scatter_dimension=0,
        tiled=True,
    )
    normed_grad = mixed_grad.reshape(shaped) * silu_gate
    inner = jnp.mean(normed_grad * normed, axis=-1, keepdims=True)
    attn_grad = (inverse * (normed_grad - normed * inner)).astype(jnp.bfloat16)
    inners = jnp.einsum("cthf,cuhf->chtu", attn_grad, value_c, preferred_element_type=jnp.float32)
    dprobs = (inners * masking).astype(jnp.bfloat16)
    qgrad = jnp.einsum("chtu,cuhe->cthe", dprobs, key_c, preferred_element_type=jnp.float32)
    kgrad = jnp.einsum("chtu,cthe->cuhe", dprobs, query_c, preferred_element_type=jnp.float32)
    vgrad = jnp.einsum("chtu,cthf->cuhf", probs, attn_grad, preferred_element_type=jnp.float32)
    weighted = (decay_in * query_c).astype(jnp.bfloat16)
    back_updates = jnp.einsum(
        "cthe,cthf->chef", weighted, attn_grad, preferred_element_type=jnp.float32
    )
    backing = jnp.zeros((head_local, HEAD_DIM, HEAD_DIM), jnp.float32)
    trailing = jnp.zeros((head_local,), jnp.float32)
    after_list = [None] * blocks
    trail_list = [None] * blocks
    for block in reversed(range(blocks)):
        after_list[block] = backing
        trail_list[block] = trailing
        backing = jnp.exp(totals[block])[:, None, None] * backing + back_updates[block]
        trailing = trailing + totals[block]
    local_after = jnp.stack(after_list)
    trail_sums = jnp.stack(trail_list)
    arriving = window_scan(jnp.exp(leading), backing, "ctx", -1)
    after_full = local_after + jnp.exp(trail_sums)[:, :, None, None] * arriving[None]
    back_b = after_full.astype(jnp.bfloat16)
    qgrad = qgrad + decay_in * jnp.einsum(
        "cthf,chef->cthe", attn_grad, rounded, preferred_element_type=jnp.float32
    )
    kgrad = kgrad + decay_out * jnp.einsum(
        "cuhf,chef->cuhe", value_c, back_b, preferred_element_type=jnp.float32
    )
    vgrad = vgrad + decay_out * jnp.einsum(
        "cuhe,chef->cuhf", key_c, back_b, preferred_element_type=jnp.float32
    )
    query_grad = qgrad.astype(jnp.bfloat16).reshape(1, tok_local, width_local)
    key_grad = kgrad.astype(jnp.bfloat16).reshape(1, tok_local, width_local)
    value_grad = vgrad.astype(jnp.bfloat16).reshape(1, tok_local, width_local)
    token_count = tok_local * lax.axis_size("ctx") * lax.axis_size("fsdp")
    grad = grad_rows / jnp.sqrt(jnp.float32(token_count))
    row_group = jnp.repeat(group_ids, ROW_BLOCK)[:, None]
    stepped = step_count[0].astype(jnp.float32)
    first = BETA_ONE * moment_one + (1.0 - BETA_ONE) * grad
    second = BETA_TWO * moment_two + (1.0 - BETA_TWO) * grad * grad
    correct_one = 1.0 - jnp.power(BETA_ONE, stepped)
    correct_two = 1.0 - jnp.power(BETA_TWO, stepped)
    active = row_group >= 1
    decayed = (row_group == 2).astype(jnp.float32)
    direction = (
        first / correct_one / (jnp.sqrt(second / correct_two) + ADAM_EPS)
        + WEIGHT_DECAY * decayed * out_weight
    )
    new_moment_one = jnp.where(active, first, moment_one)
    new_moment_two = jnp.where(active, second, moment_two)
    weight_step = jnp.where(active, direction, 0.0)
    return (query_grad, key_grad, value_grad, new_moment_one, new_moment_two, weight_step)


def solution(mesh):
    in_specs = (
        P("fsdp", "ctx", "head"),
        P("fsdp", "ctx", "head"),
        P("fsdp", "ctx", "head"),
        P("fsdp", "ctx", "head"),
        P("fsdp", "ctx", "head"),
        P("fsdp", "ctx", "head"),
        P(("ctx", "fsdp"), "head"),
        P(("ctx", "fsdp"), "head"),
        P(("ctx", "fsdp"), "head"),
        P(("ctx", "fsdp")),
        P(),
    )
    out_specs = (
        P("fsdp", "ctx", "head"),
        P("fsdp", "ctx", "head"),
        P("fsdp", "ctx", "head"),
        P(("ctx", "fsdp"), "head"),
        P(("ctx", "fsdp"), "head"),
        P(("ctx", "fsdp"), "head"),
    )
    return jax.shard_map(
        per_device, mesh=mesh, in_specs=in_specs, out_specs=out_specs, check_vma=False
    )
```

profile of v0, /device:TPU:4, one launch (start us, length us, event | category | flops | bytes accessed | tf_op | source)
XLA Modules:
  0.0 349.9 jit_solution(11883345295995269854)
XLA Ops:
  7.2 1.0 convert_element_type.66
  8.2 13.5 %all_gather.10 = bf16[256,512]{1,0:T(8,128)(2,1)} all-gather(bf16[64,512]{1,0:T(8,128)(2,1)S(1)} %convert_element_type.66), channel_id=1, replica_groups=mesh['ctx'=16,'fsdp'=4,'head'=4] {'fsdp'}, dimensions={0}, use_global_device_ids=true | all-gather | bytes 327680 | tf_op jit(solution)/shard_map/all_gather | solution.py:109
  23.3 2.4 reduce-window.6
  26.5 1.4 collective-permute-start.16
  27.9 1.3 collective-permute-start.14
  29.7 1.0 fusion.13
  30.7 0.8 fusion.28
  31.5 8.5 %collective-permute-start.4 = (f32[4,128,128]{2,1,0:T(8,128)}, f32[4,128,128]{2,1,0:T(8,128)}, u32[]{:S(2)}, u32[]{:S(2)}) collective-permute-start(f32[4,128,128]{2,1,0:T(8,128)} %fusion.28), channel_id=1, source_target_pairs={{0,48},{16,64},{32,80},{48,96},{64,112},{80,128},{96,144},{112,160... | collective-permute-start | bytes 786440 | tf_op jit(solution)/shard_map/ppermute | solution.py:25
  40.0 6.8 %collective-permute-start.2 = (f32[4,128,128]{2,1,0:T(8,128)}, f32[4,128,128]{2,1,0:T(8,128)}, u32[]{:S(2)}, u32[]{:S(2)}) collective-permute-start(f32[4,128,128]{2,1,0:T(8,128)} %fusion.28), channel_id=1, source_target_pairs={{0,32},{16,48},{32,64},{48,80},{64,96},{80,112},{96,128},{112,144}... | collective-permute-start | bytes 786440 | tf_op jit(solution)/shard_map/ppermute | solution.py:25
  46.8 3.8 %collective-permute-start = (f32[4,128,128]{2,1,0:T(8,128)}, f32[4,128,128]{2,1,0:T(8,128)}, u32[]{:S(2)}, u32[]{:S(2)}) collective-permute-start(f32[4,128,128]{2,1,0:T(8,128)} %fusion.28), channel_id=1, source_target_pairs={{0,16},{16,32},{32,48},{48,64},{64,80},{80,96},{96,112},{112,128},... | collective-permute-start | bytes 786440 | tf_op jit(solution)/shard_map/ppermute | solution.py:25
  51.8 1.0 copy-done.1
  53.4 1.3 collective-permute-start.12
  54.7 7.1 %collective-permute-start.5 = (f32[4]{0:T(128)S(1)}, f32[4]{0:T(128)S(1)}, u32[]{:S(2)}, u32[]{:S(2)}) collective-permute-start(f32[4]{0:T(128)S(1)} %get-tuple-element.40), channel_id=1, source_target_pairs={{0,48},{16,64},{32,80},{48,96},{64,112},{80,128},{96,144},{112,160... | collective-permute-start | bytes 56 | tf_op jit(solution)/shard_map/ppermute | solution.py:25
  61.9 4.3 %collective-permute-start.3 = (f32[4]{0:T(128)S(1)}, f32[4]{0:T(128)S(1)}, u32[]{:S(2)}, u32[]{:S(2)}) collective-permute-start(f32[4]{0:T(128)S(1)} %get-tuple-element.40), channel_id=1, source_target_pairs={{0,32},{16,48},{32,64},{48,80},{64,96},{80,112},{96,128},{112,144}... | collective-permute-start | bytes 56 | tf_op jit(solution)/shard_map/ppermute | solution.py:25
  66.2 22.1 %collective-permute-done.5 = f32[4]{0:T(128)S(1)} collective-permute-done((f32[4]{0:T(128)S(1)}, f32[4]{0:T(128)S(1)}, u32[]{:S(2)}, u32[]{:S(2)}) %collective-permute-start.5) | collective-permute-done | bytes 48 | tf_op jit(solution)/shard_map/ppermute | solution.py:25
  88.3 4.0 %collective-permute-start.1 = (f32[4]{0:T(128)S(1)}, f32[4]{0:T(128)S(1)}, u32[]{:S(2)}, u32[]{:S(2)}) collective-permute-start(f32[4]{0:T(128)S(1)} %get-tuple-element.40), channel_id=1, source_target_pairs={{0,16},{16,32},{32,48},{48,64},{64,80},{80,96},{96,112},{112,128},... | collective-permute-start | bytes 56 | tf_op jit(solution)/shard_map/ppermute | solution.py:25
  92.3 1.3 collective-permute-done.1
  93.6 1.0 multiply_add_fusion.6
  94.6 13.3 %collective-permute-start.10 = (f32[4,128,128]{2,1,0:T(8,128)}, f32[4,128,128]{2,1,0:T(8,128)S(1)}, u32[]{:S(2)}, u32[]{:S(2)}) collective-permute-start(f32[4,128,128]{2,1,0:T(8,128)} %get-tuple-element.55), channel_id=1, source_target_pairs={{0,192},{16,208},{32,224},{48,240},{1,193},{17,209},{33,225},{49,2... | collective-permute-start | bytes 786440 | tf_op jit(solution)/shard_map/ppermute | solution.py:25
  107.9 3.0 collective-permute-start.8
  110.9 2.2 collective-permute-start.6
  113.1 2.4 reshape.180
  115.5 2.5 copy.192
  118.1 1.3 collective-permute-start.9
  119.3 5.7 %collective-permute-start.7 = (f32[4]{0:T(128)S(1)}, f32[4]{0:T(128)S(1)}, u32[]{:S(2)}, u32[]{:S(2)}) collective-permute-start(f32[4]{0:T(128)S(1)} %get-tuple-element.64), channel_id=1, source_target_pairs={{0,64},{16,80},{32,96},{48,112},{64,128},{80,144},{96,160},{112,17... | collective-permute-start | bytes 56 | tf_op jit(solution)/shard_map/ppermute | solution.py:25
  125.0 8.0 %collective-permute-done.7 = f32[4]{0:T(128)S(1)} collective-permute-done((f32[4]{0:T(128)S(1)}, f32[4]{0:T(128)S(1)}, u32[]{:S(2)}, u32[]{:S(2)}) %collective-permute-start.7) | collective-permute-done | bytes 48 | tf_op jit(solution)/shard_map/ppermute | solution.py:25
  133.9 1.5 multiply_reduce_fusion.1
  135.4 3.5 all-gather.5.cloned.1.call-done
  138.9 6.5 %copy.190 = bf16[512,4096]{1,0:T(8,128)(2,1)} copy(bf16[512,4096]{0,1:T(8,128)(2,1)} %bitcast.113) | data formatting | bytes 8388608 | tf_op jit(solution)/shard_map/dot_general | solution.py:106
  145.4 33.7 %all-gather.3.cloned.1.call-done = bf16[1,512,4096]{2,1,0:T(8,128)(2,1)} async-done(((bf16[1,512,1024]{2,1,0:T(8,128)(2,1)}), bf16[1,512,4096]{2,1,0:T(8,128)(2,1)}) %all-gather.3.cloned.1.call-update) | async-done | bytes 4194320 | tf_op jit(solution)/shard_map/all_gather | solution.py:103
  179.1 6.3 %multiply_reduce_fusion = (f32[2,256,4]{1,2,0:T(4,128)S(1)}, f32[2,256,4,128]{1,3,2,0:T(8,128)S(1)}) fusion(f32[2,256,4,128]{1,3,2,0:T(8,128)} %get-tuple-element.69, f32[2,256,4]{1,2,0:T(4,128)S(1)} %add_rsqrt_fusion, f32[2,256,4,128]{1,3,2,0:T(8,128)S(1)} %copy-done.3, bf16[2,256,4096,1]{2,1,3,0:T(8,128)(2,1)} %bitcast.112, ...), kind=kOutput, calls=%fused_computation.29 | convolution fusion | flops 2149578752 | bytes 11550720 | tf_op jit(solution)/shard_map/dot_general | solution.py:106
  185.4 1.2 multiply_convert_fusion.2
  186.7 1.3 copy.212
  188.0 6.6 %fusion = bf16[4096,512]{0,1:T(8,128)(2,1)} fusion(bf16[1,512,4096]{2,1,0:T(8,128)(2,1)} %all-gather.3.cloned.1.call-done, bf16[64,8,4,128]{3,2,1,0:T(4,128)(2,1)S(1)} %bitcast.115), kind=kOutput, calls=%fused_computation.1 | convolution fusion | flops 2149580800 | bytes 8912896 | tf_op jit(solution)/shard_map/td,th->dh/dot_general | solution.py:116
  194.7 0.8 copy-done.12
  195.5 0.9 copy.216
  197.4 0.8 copy.211
  198.3 0.8 copy.214
  199.1 1.3 collective-permute-start.20
  200.4 1.3 collective-permute-start.18
  201.7 2.9 collective-permute-done.20
  204.6 5.2 %collective-permute-done.18 = f32[4]{0:T(128)S(1)} collective-permute-done((f32[4]{0:T(128)S(1)}, f32[4]{0:T(128)S(1)}, u32[]{:S(2)}, u32[]{:S(2)}) %collective-permute-start.18) | collective-permute-done | bytes 48 | tf_op jit(solution)/shard_map/ppermute | solution.py:25
  210.2 1.4 collective-permute-start.15
  211.6 1.3 collective-permute-start.13
  212.9 1.5 collective-permute-start.11
  214.4 1.6 multiply_convert_fusion
  216.1 1.5 convolution_bitcast_fusion.4
  217.6 1.5 convolution_bitcast_fusion.5
  219.5 20.3 %collective-permute-done.15 = f32[4,128,128]{2,1,0:T(8,128)S(1)} collective-permute-done((f32[4,128,128]{2,1,0:T(8,128)S(1)}, f32[4,128,128]{2,1,0:T(8,128)S(1)}, u32[]{:S(2)}, u32[]{:S(2)}) %collective-permute-start.15) | collective-permute-done | bytes 262176 | tf_op jit(solution)/shard_map/ppermute | solution.py:25
  240.4 1.0 multiply_add_fusion.3
  241.4 1.3 collective-permute-start.21
  242.6 1.3 collective-permute-start.19
  243.9 1.3 collective-permute-start.17
  245.9 1.0 reshape.176
  246.9 68.4 %reduce-scatter.5.cloned.1.call-done = bf16[256,512]{0,1:T(8,128)(2,1)} async-done(((bf16[4096,512]{0,1:T(8,128)(2,1)}), bf16[256,512]{0,1:T(8,128)(2,1)}) %reduce-scatter.5.cloned.1.call-update) | async-done | bytes 262160 | tf_op jit(solution)/shard_map/reduce_scatter | solution.py:115
  315.3 1.9 copy.233
  317.4 1.2 multiply_add_fusion.2
  318.7 1.7 fusion.12
  320.8 1.0 reshape.178
  322.6 1.0 reshape.177
  323.6 16.2 %reduce-scatter.7.cloned.1.call-done = f32[64,512]{1,0:T(8,128)} async-done(((f32[256,512]{1,0:T(8,128)}), f32[64,512]{1,0:T(8,128)}) %reduce-scatter.7.cloned.1.call-update) | async-done | bytes 131088
  339.7 1.0 copy.234
  341.0 0.8 copy.219
  341.8 0.8 copy.218
  (112 shorter events, 10.2 us)
Async XLA Ops:
  7.2 22.0 %copy-start.13 = (bf16[1,512,512]{2,1,0:T(8,128)(2,1)S(1)}, bf16[1,512,512]{2,1,0:T(8,128)(2,1)}, u32[]{:S(2)}) copy-start(bf16[1,512,512]{2,1,0:T(8,128)(2,1)} %param.12) | copy-start | bytes 1572868
  7.2 22.2 %copy-start.14 = (bf16[1,512,512]{2,1,0:T(8,128)(2,1)S(1)}, bf16[1,512,512]{2,1,0:T(8,128)(2,1)}, u32[]{:S(2)}) copy-start(bf16[1,512,512]{2,1,0:T(8,128)(2,1)} %param.13) | copy-start | bytes 1572868
  7.2 131.7 %all-gather.5.cloned.1.call-start = ((), (), s32[]{:S(2)}) async-start(), calls=%async_computation.3 | async-start | bytes 4456448 | tf_op jit(solution)/shard_map/all_gather | solution.py:108
  21.8 157.3 %all-gather.3.cloned.1.call-start = ((), (), s32[]{:S(2)}) async-start(), calls=%async_computation.2 | async-start | bytes 5242880 | tf_op jit(solution)/shard_map/all_gather | solution.py:103
  22.5 292.8 %reduce-scatter.5.cloned.1.call-start = ((), (), s32[]{:S(2)}) async-start(), calls=%async_computation.4 | async-start | bytes 4456448 | tf_op jit(solution)/shard_map/reduce_scatter | solution.py:115
  26.4 24.2 %copy-start.15 = (bf16[1,512,512]{2,1,0:T(8,128)(2,1)S(1)}, bf16[1,512,512]{2,1,0:T(8,128)(2,1)}, u32[]{:S(2)}) copy-start(bf16[1,512,512]{2,1,0:T(8,128)(2,1)} %param.11) | copy-start | bytes 1572868
  26.5 27.0 %collective-permute-start.16 = (f32[4]{0:T(128)S(1)}, f32[4]{0:T(128)S(1)}, u32[]{:S(2)}, u32[]{:S(2)}) collective-permute-start(f32[4]{0:T(128)S(1)} %get-tuple-element.40), channel_id=1, source_target_pairs={{48,0},{64,16},{80,32},{96,48},{112,64},{128,80},{144,96},{160,112... | collective-permute-start | bytes 56 | tf_op jit(solution)/shard_map/ppermute | solution.py:25
  27.9 26.8 %collective-permute-start.14 = (f32[4]{0:T(128)S(1)}, f32[4]{0:T(128)S(1)}, u32[]{:S(2)}, u32[]{:S(2)}) collective-permute-start(f32[4]{0:T(128)S(1)} %get-tuple-element.40), channel_id=1, source_target_pairs={{32,0},{48,16},{64,32},{80,48},{96,64},{112,80},{128,96},{144,112}... | collective-permute-start | bytes 56 | tf_op jit(solution)/shard_map/ppermute | solution.py:25
  31.5 62.0 %collective-permute-start.4 = (f32[4,128,128]{2,1,0:T(8,128)}, f32[4,128,128]{2,1,0:T(8,128)}, u32[]{:S(2)}, u32[]{:S(2)}) collective-permute-start(f32[4,128,128]{2,1,0:T(8,128)} %fusion.28), channel_id=1, source_target_pairs={{0,48},{16,64},{32,80},{48,96},{64,112},{80,128},{96,144},{112,160... | collective-permute-start | bytes 786440 | tf_op jit(solution)/shard_map/ppermute | solution.py:25
  40.0 53.5 %collective-permute-start.2 = (f32[4,128,128]{2,1,0:T(8,128)}, f32[4,128,128]{2,1,0:T(8,128)}, u32[]{:S(2)}, u32[]{:S(2)}) collective-permute-start(f32[4,128,128]{2,1,0:T(8,128)} %fusion.28), channel_id=1, source_target_pairs={{0,32},{16,48},{32,64},{48,80},{64,96},{80,112},{96,128},{112,144}... | collective-permute-start | bytes 786440 | tf_op jit(solution)/shard_map/ppermute | solution.py:25
  46.8 46.8 %collective-permute-start = (f32[4,128,128]{2,1,0:T(8,128)}, f32[4,128,128]{2,1,0:T(8,128)}, u32[]{:S(2)}, u32[]{:S(2)}) collective-permute-start(f32[4,128,128]{2,1,0:T(8,128)} %fusion.28), channel_id=1, source_target_pairs={{0,16},{16,32},{32,48},{48,64},{64,80},{80,96},{96,112},{112,128},... | collective-permute-start | bytes 786440 | tf_op jit(solution)/shard_map/ppermute | solution.py:25
  51.1 2.2 copy-start.16
  51.8 1.0 copy-start.1
  53.4 8.5 %collective-permute-start.12 = (f32[4]{0:T(128)S(1)}, f32[4]{0:T(128)S(1)}, u32[]{:S(2)}, u32[]{:S(2)}) collective-permute-start(f32[4]{0:T(128)S(1)} %get-tuple-element.40), channel_id=1, source_target_pairs={{16,0},{32,16},{48,32},{64,48},{80,64},{96,80},{112,96},{128,112},... | collective-permute-start | bytes 56 | tf_op jit(solution)/shard_map/ppermute | solution.py:25
  54.7 33.5 %collective-permute-start.5 = (f32[4]{0:T(128)S(1)}, f32[4]{0:T(128)S(1)}, u32[]{:S(2)}, u32[]{:S(2)}) collective-permute-start(f32[4]{0:T(128)S(1)} %get-tuple-element.40), channel_id=1, source_target_pairs={{0,48},{16,64},{32,80},{48,96},{64,112},{80,128},{96,144},{112,160... | collective-permute-start | bytes 56 | tf_op jit(solution)/shard_map/ppermute | solution.py:25
  61.9 30.4 %collective-permute-start.3 = (f32[4]{0:T(128)S(1)}, f32[4]{0:T(128)S(1)}, u32[]{:S(2)}, u32[]{:S(2)}) collective-permute-start(f32[4]{0:T(128)S(1)} %get-tuple-element.40), channel_id=1, source_target_pairs={{0,32},{16,48},{32,64},{48,80},{64,96},{80,112},{96,128},{112,144}... | collective-permute-start | bytes 56 | tf_op jit(solution)/shard_map/ppermute | solution.py:25
  88.3 5.3 %collective-permute-start.1 = (f32[4]{0:T(128)S(1)}, f32[4]{0:T(128)S(1)}, u32[]{:S(2)}, u32[]{:S(2)}) collective-permute-start(f32[4]{0:T(128)S(1)} %get-tuple-element.40), channel_id=1, source_target_pairs={{0,16},{16,32},{32,48},{48,64},{64,80},{80,96},{96,112},{112,128},... | collective-permute-start | bytes 56 | tf_op jit(solution)/shard_map/ppermute | solution.py:25
  94.6 39.2 %copy-start.7 = (f32[4,128,128]{2,1,0:T(8,128)S(1)}, f32[4,128,128]{2,1,0:T(8,128)}, u32[]{:S(2)}) copy-start(f32[4,128,128]{2,1,0:T(8,128)} %get-tuple-element.56) | copy-start | bytes 786436
  94.6 38.5 %collective-permute-start.10 = (f32[4,128,128]{2,1,0:T(8,128)}, f32[4,128,128]{2,1,0:T(8,128)S(1)}, u32[]{:S(2)}, u32[]{:S(2)}) collective-permute-start(f32[4,128,128]{2,1,0:T(8,128)} %get-tuple-element.55), channel_id=1, source_target_pairs={{0,192},{16,208},{32,224},{48,240},{1,193},{17,209},{33,225},{49,2... | collective-permute-start | bytes 786440 | tf_op jit(solution)/shard_map/ppermute | solution.py:25
  107.9 25.1 %collective-permute-start.8 = (f32[4,128,128]{2,1,0:T(8,128)}, f32[4,128,128]{2,1,0:T(8,128)}, u32[]{:S(2)}, u32[]{:S(2)}) collective-permute-start(f32[4,128,128]{2,1,0:T(8,128)} %get-tuple-element.55), channel_id=1, source_target_pairs={{0,128},{16,144},{32,160},{48,176},{64,192},{80,208},{96,224},{112... | collective-permute-start | bytes 786440 | tf_op jit(solution)/shard_map/ppermute | solution.py:25
  110.9 22.2 %collective-permute-start.6 = (f32[4,128,128]{2,1,0:T(8,128)}, f32[4,128,128]{2,1,0:T(8,128)}, u32[]{:S(2)}, u32[]{:S(2)}) collective-permute-start(f32[4,128,128]{2,1,0:T(8,128)} %get-tuple-element.55), channel_id=1, source_target_pairs={{0,64},{16,80},{32,96},{48,112},{64,128},{80,144},{96,160},{112,17... | collective-permute-start | bytes 786440 | tf_op jit(solution)/shard_map/ppermute | solution.py:25
  118.1 7.0 %collective-permute-start.9 = (f32[4]{0:T(128)S(1)}, f32[4]{0:T(128)S(1)}, u32[]{:S(2)}, u32[]{:S(2)}) collective-permute-start(f32[4]{0:T(128)S(1)} %get-tuple-element.64), channel_id=1, source_target_pairs={{0,128},{16,144},{32,160},{48,176},{64,192},{80,208},{96,224},{112... | collective-permute-start | bytes 56 | tf_op jit(solution)/shard_map/ppermute | solution.py:25
  119.3 13.7 %collective-permute-start.7 = (f32[4]{0:T(128)S(1)}, f32[4]{0:T(128)S(1)}, u32[]{:S(2)}, u32[]{:S(2)}) collective-permute-start(f32[4]{0:T(128)S(1)} %get-tuple-element.64), channel_id=1, source_target_pairs={{0,64},{16,80},{32,96},{48,112},{64,128},{80,144},{96,160},{112,17... | collective-permute-start | bytes 56 | tf_op jit(solution)/shard_map/ppermute | solution.py:25
  133.0 0.7 copy-start.17
  133.9 5.0 %copy-start.5 = (f32[4,128,128]{2,1,0:T(8,128)}, f32[4,128,128]{2,1,0:T(8,128)S(1)}, u32[]{:S(2)}) copy-start(f32[4,128,128]{2,1,0:T(8,128)S(1)} %multiply_add_fusion.5) | copy-start | bytes 786436
  138.9 40.2 %copy-start.3 = (f32[2,256,4,128]{1,3,2,0:T(8,128)S(1)}, f32[2,256,4,128]{1,3,2,0:T(8,128)}, u32[]{:S(2)}) copy-start(f32[2,256,4,128]{1,3,2,0:T(8,128)} %copy.192) | copy-start | bytes 3145732
  179.1 6.3 %copy-start.4 = (f32[2,256,4,128]{1,3,2,0:T(8,128)S(1)}, f32[2,256,4,128]{1,3,2,0:T(8,128)}, u32[]{:S(2)}) copy-start(f32[2,256,4,128]{1,3,2,0:T(8,128)} %get-tuple-element.69) | copy-start | bytes 3145732
  194.6 0.9 copy-start.12
  194.6 2.5 copy-start.20
  194.6 2.8 copy-start.18
  194.6 3.7 %copy-start.19 = (f32[64,512]{1,0:T(8,128)S(1)}, f32[64,512]{1,0:T(8,128)}, u32[]{:S(2)}) copy-start(f32[64,512]{1,0:T(8,128)} %param.19) | copy-start | bytes 393220
  194.6 145.1 %reduce-scatter.7.cloned.1.call-start = ((), (), s32[]{:S(2)}) async-start(), calls=%async_computation.5 | async-start | bytes 655360
  199.1 5.5 %collective-permute-start.20 = (f32[4]{0:T(128)S(1)}, f32[4]{0:T(128)S(1)}, u32[]{:S(2)}, u32[]{:S(2)}) collective-permute-start(f32[4]{0:T(128)S(1)} %get-tuple-element.43), channel_id=1, source_target_pairs={{128,0},{144,16},{160,32},{176,48},{192,64},{208,80},{224,96},{240... | collective-permute-start | bytes 56 | tf_op jit(solution)/shard_map/ppermute | solution.py:25
  200.4 9.4 %collective-permute-start.18 = (f32[4]{0:T(128)S(1)}, f32[4]{0:T(128)S(1)}, u32[]{:S(2)}, u32[]{:S(2)}) collective-permute-start(f32[4]{0:T(128)S(1)} %get-tuple-element.43), channel_id=1, source_target_pairs={{64,0},{80,16},{96,32},{112,48},{128,64},{144,80},{160,96},{176,11... | collective-permute-start | bytes 56 | tf_op jit(solution)/shard_map/ppermute | solution.py:25
  210.1 6.0 %copy-start.2 = (bf16[2,4,256,256]{3,2,1,0:T(8,128)(2,1)S(1)}, bf16[2,4,256,256]{3,2,1,0:T(8,128)(2,1)}, u32[]{:S(2)}) copy-start(bf16[2,4,256,256]{3,2,1,0:T(8,128)(2,1)} %copy-done.1) | copy-start | bytes 3145732
  210.2 29.6 %collective-permute-start.15 = (f32[4,128,128]{2,1,0:T(8,128)S(1)}, f32[4,128,128]{2,1,0:T(8,128)S(1)}, u32[]{:S(2)}, u32[]{:S(2)}) collective-permute-start(f32[4,128,128]{2,1,0:T(8,128)S(1)} %fusion.27), channel_id=1, source_target_pairs={{48,0},{64,16},{80,32},{96,48},{112,64},{128,80},{144,96},{160,112... | collective-permute-start | bytes 786440 | tf_op jit(solution)/shard_map/ppermute | solution.py:25
  211.6 28.7 %collective-permute-start.13 = (f32[4,128,128]{2,1,0:T(8,128)S(1)}, f32[4,128,128]{2,1,0:T(8,128)S(1)}, u32[]{:S(2)}, u32[]{:S(2)}) collective-permute-start(f32[4,128,128]{2,1,0:T(8,128)S(1)} %fusion.27), channel_id=1, source_target_pairs={{32,0},{48,16},{64,32},{80,48},{96,64},{112,80},{128,96},{144,112}... | collective-permute-start | bytes 786440 | tf_op jit(solution)/shard_map/ppermute | solution.py:25
  212.9 27.5 %collective-permute-start.11 = (f32[4,128,128]{2,1,0:T(8,128)S(1)}, f32[4,128,128]{2,1,0:T(8,128)S(1)}, u32[]{:S(2)}, u32[]{:S(2)}) collective-permute-start(f32[4,128,128]{2,1,0:T(8,128)S(1)} %fusion.27), channel_id=1, source_target_pairs={{16,0},{32,16},{48,32},{64,48},{80,64},{96,80},{112,96},{128,112},... | collective-permute-start | bytes 786440 | tf_op jit(solution)/shard_map/ppermute | solution.py:25
  219.0 26.2 %copy-start.6 = (f32[4,128,128]{2,1,0:T(8,128)S(1)}, f32[4,128,128]{2,1,0:T(8,128)}, u32[]{:S(2)}) copy-start(f32[4,128,128]{2,1,0:T(8,128)} %copy-done.5) | copy-start | bytes 786436
  241.4 76.0 %collective-permute-start.21 = (f32[4,128,128]{2,1,0:T(8,128)}, f32[4,128,128]{2,1,0:T(8,128)}, u32[]{:S(2)}, u32[]{:S(2)}) collective-permute-start(f32[4,128,128]{2,1,0:T(8,128)} %get-tuple-element.47), channel_id=1, source_target_pairs={{192,0},{208,16},{224,32},{240,48},{193,1},{209,17},{225,33},{241,... | collective-permute-start | bytes 786440 | tf_op jit(solution)/shard_map/ppermute | solution.py:25
  242.6 74.7 %collective-permute-start.19 = (f32[4,128,128]{2,1,0:T(8,128)}, f32[4,128,128]{2,1,0:T(8,128)}, u32[]{:S(2)}, u32[]{:S(2)}) collective-permute-start(f32[4,128,128]{2,1,0:T(8,128)} %get-tuple-element.47), channel_id=1, source_target_pairs={{128,0},{144,16},{160,32},{176,48},{192,64},{208,80},{224,96},{240... | collective-permute-start | bytes 786440 | tf_op jit(solution)/shard_map/ppermute | solution.py:25
  243.9 73.4 %collective-permute-start.17 = (f32[4,128,128]{2,1,0:T(8,128)}, f32[4,128,128]{2,1,0:T(8,128)}, u32[]{:S(2)}, u32[]{:S(2)}) collective-permute-start(f32[4,128,128]{2,1,0:T(8,128)} %get-tuple-element.47), channel_id=1, source_target_pairs={{64,0},{80,16},{96,32},{112,48},{128,64},{144,80},{160,96},{176,11... | collective-permute-start | bytes 786440 | tf_op jit(solution)/shard_map/ppermute | solution.py:25
  245.6 71.8 %copy-start.8 = (f32[4,128,128]{2,1,0:T(8,128)S(1)}, f32[4,128,128]{2,1,0:T(8,128)}, u32[]{:S(2)}) copy-start(f32[4,128,128]{2,1,0:T(8,128)} %get-tuple-element.48) | copy-start | bytes 786436
  318.7 3.1 copy-start
  321.8 19.0 %copy-start.9 = (f32[64,512]{0,1:T(8,128)S(1)}, f32[64,512]{0,1:T(8,128)}, u32[]{:S(2)}) copy-start(f32[64,512]{0,1:T(8,128)} %copy.216) | copy-start | bytes 393220
  321.8 19.0 %copy-start.10 = (f32[64,512]{0,1:T(8,128)S(1)}, f32[64,512]{0,1:T(8,128)}, u32[]{:S(2)}) copy-start(f32[64,512]{0,1:T(8,128)} %copy.211) | copy-start | bytes 393220
  321.8 19.0 %copy-start.11 = (f32[64,512]{0,1:T(8,128)S(1)}, f32[64,512]{0,1:T(8,128)}, u32[]{:S(2)}) copy-start(f32[64,512]{0,1:T(8,128)} %copy.214) | copy-start | bytes 393220
Sparse Core Ops, SparseCore 0:
  21.9 116.9 all-gather.4
  140.7 38.3 all-gather.2
  194.7 120.5 reduce-scatter.4
  317.7 21.9 reduce-scatter.6
where the time goes:
time: 351 us; the launch traced here: 350 us
  waiting for transfers between devices  183 us (52%)
  starting transfers between devices  74.7 us (21%)
  local copies, waits for them, and re-layouts  29.4 us (8%)
  matrix products  24.4 us (7%)
  between operations  15.2 us (4%)
  blocking collectives  13.5 us (4%)
  other arithmetic  9.79 us (3%)
    ppermute x22, starting transfers between devices, fetch(): got = lax.ppermute(value, axis, pairs)  74.6 us
    reduce_scatter x1, waiting for transfers between devices, per_device(): lax.psum_scatter(jnp.einsum('td,th->dh', columns, mixed, preferred_elemen...  68.4 us
    ppermute x22, waiting for transfers between devices, fetch(): got = lax.ppermute(value, axis, pairs)  60.4 us
    all_gather x1, waiting for transfers between devices, per_device(): features = lax.all_gather(out_grad, 'head', axis=2, tiled=True)[0]  33.7 us
    unnamed x5, waiting for transfers between devices  16.9 us
    all_gather x1, blocking collectives, per_device(): lax.all_gather(weight_b, 'fsdp', axis=0, tiled=True)  13.5 us
    unnamed x50, local copies, waits for them, and re-layouts  10.3 us
  transfers between devices with their start and end apart: 26, of which 11 were waited for; matrix products, arithmetic and copies ran while one was open for 12% of the time, Pallas kernels for 0%

commit v1 on v0

--- a/solution.py
+++ b/solution.py
@@ -11,6 +11,30 @@
 BETA_TWO = 0.95
 ADAM_EPS = 1e-08
 WEIGHT_DECAY = 0.1
+
+
+def watch_the_vector(x_local):
+    axis_name = "fsdp"
+    formed = jax.lax.axis_size(axis_name)
+    current_block = jax.lax.axis_index(axis_name)
+    d_next, tmp, z2 = (formed, current_block, x_local.shape[0])
+    sides = []
+    for idx in range(d_next):
+        sides.append((idx, (idx + 1) % d_next))
+    series = []
+    for idx in range(d_next):
+        series.append((idx, (idx - 1) % d_next))
+    h_now = jnp.zeros((*x_local.shape[:0], d_next * z2, *x_local.shape[1:]), x_local.dtype)
+    h_now = lax.dynamic_update_slice_in_dim(h_now, x_local, tmp * z2, axis=0)
+    res = y2 = x_local
+    u1 = d_next // 2
+    for rr in range(1, u1 + 1):
+        res = jax.lax.ppermute(res, axis_name, sides)
+        h_now = lax.dynamic_update_slice_in_dim(h_now, res, (tmp - rr) % d_next * z2, axis=0)
+        if rr < d_next - u1:
+            y2 = jax.lax.ppermute(y2, axis_name, series)
+            h_now = lax.dynamic_update_slice_in_dim(h_now, y2, (tmp + rr) % d_next * z2, axis=0)
+    return h_now
 
 
 def window_scan(gain, state, axis, sign):
@@ -105,9 +129,7 @@
     columns = features
     mixed_grad = jnp.dot(
         columns,
-        lax.all_gather(
-            lax.all_gather(weight_b, "fsdp", axis=0, tiled=True), "ctx", axis=0, tiled=True
-        ),
+        lax.all_gather(watch_the_vector(weight_b), "ctx", axis=0, tiled=True),
         preferred_element_type=jnp.float32,
     )
     columns = features

time: 351 us -> 320 us (0.912)
  waiting for transfers between devices: 183 us -> 169 us
  blocking collectives: 13.5 us -> 0 us
  local copies, waits for them, and re-layouts: 29.4 us -> 19.5 us
  starting transfers between devices: 74.7 us -> 80.5 us
    all_gather x1, waiting for transfers between devices: 33.7 us -> 0.02 us  [per_device(): features = lax.all_gather(out_grad, 'head', axis=2, tiled=True)[0]]
    all_gather x1, waiting for transfers between devices: 3.49 us -> 27.7 us  [per_device(): lax.all_gather(watch_the_vector(weight_b), 'ctx', axis=0, tiled=True)]
    all_gather x1 -> x0, blocking collectives: 13.5 us -> none  [per_device(): lax.all_gather(weight_b, 'fsdp', axis=0, tiled=True)]
    ppermute x22, waiting for transfers between devices: 60.4 us -> 49.9 us  [fetch(): got = lax.ppermute(value, axis, pairs)]
    ppermute x0 -> x3, waiting for transfers between devices: none -> 7.31 us  [the longest x2 7.31 us: watch_the_vector(): res = jax.lax.ppermute(res, axis_name, sides)]
    dot_general x1 -> x0, local copies, waits for them, and re-layouts: 6.49 us -> none  [per_device(): jnp.dot(columns, lax.all_gather(lax.all_gather(weight_b, 'fsdp', axis=0,...]
    convert_element_type x2, local copies, waits for them, and re-layouts: 4.97 us -> 0.68 us  [per_device(): silu_gate = jax.nn.silu(gate_pre.reshape(shaped).astype(jnp.float32))]
    reduce_scatter x1, waiting for transfers between devices: 68.4 us -> 64.2 us  [per_device(): lax.psum_scatter(jnp.einsum('td,th->dh', columns, mixed, preferred_elemen...]
  transfers between devices with their start and end apart: 26 -> 29, of which waited for: 11 -> 12; matrix products, arithmetic and copies ran while one was open for 12% -> 10% of each run, Pallas kernels for 0% -> 0%
where the time goes in v1:
time: 320 us; the launch traced here: 319 us
  waiting for transfers between devices  169 us (53%)
  starting transfers between devices  80.5 us (25%)
  matrix products  25.3 us (8%)
  local copies, waits for them, and re-layouts  19.5 us (6%)
  between operations  15.3 us (5%)
  other arithmetic  10.2 us (3%)
    ppermute x22, starting transfers between devices, fetch(): got = lax.ppermute(value, axis, pairs)  76.6 us
    reduce_scatter x1, waiting for transfers between devices, per_device(): lax.psum_scatter(jnp.einsum('td,th->dh', columns, mixed, preferred_elemen...  64.2 us
    ppermute x22, waiting for transfers between devices, fetch(): got = lax.ppermute(value, axis, pairs)  49.9 us
    all_gather x1, waiting for transfers between devices, per_device(): lax.all_gather(watch_the_vector(weight_b), 'ctx', axis=0, tiled=True)  27.7 us
    unnamed x5, waiting for transfers between devices  19.4 us
    unnamed x66, local copies, waits for them, and re-layouts  10 us
    ppermute x2, waiting for transfers between devices, watch_the_vector(): res = jax.lax.ppermute(res, axis_name, sides)  7.31 us
    dot_general x1, matrix products, per_device(): jnp.dot(columns, lax.all_gather(watch_the_vector(weight_b), 'ctx', axis=0...  6.83 us
  transfers between devices with their start and end apart: 29, of which 12 were waited for; matrix products, arithmetic and copies ran while one was open for 10% of the time, Pallas kernels for 0%

profile of v1, /device:TPU:4, one launch (start us, length us, event | category | flops | bytes accessed | tf_op | source)
XLA Modules:
  0.0 319.4 jit_solution(17071280351191995608)
XLA Ops:
  8.0 0.9 constant_dynamic-update-slice_fusion.3
  8.9 1.7 collective-permute-start.11
  10.6 1.7 collective-permute-start.12
  12.3 2.2 collective-permute-done.11
  14.9 5.1 %collective-permute-done.13 = bf16[64,512]{1,0:T(8,128)(2,1)S(1)} collective-permute-done((bf16[64,512]{1,0:T(8,128)(2,1)S(1)}, bf16[64,512]{1,0:T(8,128)(2,1)S(1)}, u32[]{:S(2)}, u32[]{:S(2)}) %collective-permute-start.13) | collective-permute-done | bytes 65568 | tf_op jit(solution)/shard_map/ppermute | solution.py:32
  20.8 2.4 reduce-window.6
  24.0 1.4 collective-permute-start.19
  25.4 1.3 collective-permute-start.17
  27.2 1.0 fusion.18
  28.3 0.8 fusion.33
  29.1 8.5 %collective-permute-start.4 = (f32[4,128,128]{2,1,0:T(8,128)}, f32[4,128,128]{2,1,0:T(8,128)}, u32[]{:S(2)}, u32[]{:S(2)}) collective-permute-start(f32[4,128,128]{2,1,0:T(8,128)} %fusion.33), channel_id=1, source_target_pairs={{0,48},{16,64},{32,80},{48,96},{64,112},{80,128},{96,144},{112,160... | collective-permute-start | bytes 786440 | tf_op jit(solution)/shard_map/ppermute | solution.py:49
  37.5 6.7 %collective-permute-start.2 = (f32[4,128,128]{2,1,0:T(8,128)}, f32[4,128,128]{2,1,0:T(8,128)}, u32[]{:S(2)}, u32[]{:S(2)}) collective-permute-start(f32[4,128,128]{2,1,0:T(8,128)} %fusion.33), channel_id=1, source_target_pairs={{0,32},{16,48},{32,64},{48,80},{64,96},{80,112},{96,128},{112,144}... | collective-permute-start | bytes 786440 | tf_op jit(solution)/shard_map/ppermute | solution.py:49
  44.3 3.9 %collective-permute-start = (f32[4,128,128]{2,1,0:T(8,128)}, f32[4,128,128]{2,1,0:T(8,128)}, u32[]{:S(2)}, u32[]{:S(2)}) collective-permute-start(f32[4,128,128]{2,1,0:T(8,128)} %fusion.33), channel_id=1, source_target_pairs={{0,16},{16,32},{32,48},{48,64},{64,80},{80,96},{96,112},{112,128},... | collective-permute-start | bytes 786440 | tf_op jit(solution)/shard_map/ppermute | solution.py:49
  49.4 1.5 convolution_bitcast_fusion.7
  51.0 1.3 collective-permute-start.15
  52.3 7.1 %collective-permute-start.5 = (f32[4]{0:T(128)S(1)}, f32[4]{0:T(128)S(1)}, u32[]{:S(2)}, u32[]{:S(2)}) collective-permute-start(f32[4]{0:T(128)S(1)} %get-tuple-element.40), channel_id=1, source_target_pairs={{0,48},{16,64},{32,80},{48,96},{64,112},{80,128},{96,144},{112,160... | collective-permute-start | bytes 56 | tf_op jit(solution)/shard_map/ppermute | solution.py:49
  59.4 4.3 %collective-permute-start.3 = (f32[4]{0:T(128)S(1)}, f32[4]{0:T(128)S(1)}, u32[]{:S(2)}, u32[]{:S(2)}) collective-permute-start(f32[4]{0:T(128)S(1)} %get-tuple-element.40), channel_id=1, source_target_pairs={{0,32},{16,48},{32,64},{48,80},{64,96},{80,112},{96,128},{112,144}... | collective-permute-start | bytes 56 | tf_op jit(solution)/shard_map/ppermute | solution.py:49
  63.7 6.3 %collective-permute-done.5 = f32[4]{0:T(128)S(1)} collective-permute-done((f32[4]{0:T(128)S(1)}, f32[4]{0:T(128)S(1)}, u32[]{:S(2)}, u32[]{:S(2)}) %collective-permute-start.5) | collective-permute-done | bytes 48 | tf_op jit(solution)/shard_map/ppermute | solution.py:49
  70.0 3.6 %collective-permute-start.1 = (f32[4]{0:T(128)S(1)}, f32[4]{0:T(128)S(1)}, u32[]{:S(2)}, u32[]{:S(2)}) collective-permute-start(f32[4]{0:T(128)S(1)} %get-tuple-element.40), channel_id=1, source_target_pairs={{0,16},{16,32},{32,48},{48,64},{64,80},{80,96},{96,112},{112,128},... | collective-permute-start | bytes 56 | tf_op jit(solution)/shard_map/ppermute | solution.py:49
  73.6 1.3 collective-permute-done.1
  74.9 1.0 multiply_add_fusion.6
  75.9 17.3 %collective-permute-start.10 = (f32[4,128,128]{2,1,0:T(8,128)}, f32[4,128,128]{2,1,0:T(8,128)S(1)}, u32[]{:S(2)}, u32[]{:S(2)}) collective-permute-start(f32[4,128,128]{2,1,0:T(8,128)} %get-tuple-element.57), channel_id=1, source_target_pairs={{0,192},{16,208},{32,224},{48,240},{1,193},{17,209},{33,225},{49,2... | collective-permute-start | bytes 786440 | tf_op jit(solution)/shard_map/ppermute | solution.py:49
  93.2 2.0 collective-permute-start.8
  95.2 3.2 collective-permute-start.6
  99.1 1.3 collective-permute-start.9
  100.4 4.0 %collective-permute-start.7 = (f32[4]{0:T(128)S(1)}, f32[4]{0:T(128)S(1)}, u32[]{:S(2)}, u32[]{:S(2)}) collective-permute-start(f32[4]{0:T(128)S(1)} %get-tuple-element.66), channel_id=1, source_target_pairs={{0,64},{16,80},{32,96},{48,112},{64,128},{80,144},{96,160},{112,17... | collective-permute-start | bytes 56 | tf_op jit(solution)/shard_map/ppermute | solution.py:49
  104.5 4.1 %collective-permute-done.9 = f32[4]{0:T(128)S(1)} collective-permute-done((f32[4]{0:T(128)S(1)}, f32[4]{0:T(128)S(1)}, u32[]{:S(2)}, u32[]{:S(2)}) %collective-permute-start.9) | collective-permute-done | bytes 48 | tf_op jit(solution)/shard_map/ppermute | solution.py:49
  108.6 10.0 %collective-permute-done.7 = f32[4]{0:T(128)S(1)} collective-permute-done((f32[4]{0:T(128)S(1)}, f32[4]{0:T(128)S(1)}, u32[]{:S(2)}, u32[]{:S(2)}) %collective-permute-start.7) | collective-permute-done | bytes 48 | tf_op jit(solution)/shard_map/ppermute | solution.py:49
  119.5 1.8 multiply_reduce_fusion.1
  121.4 27.7 %all-gather.3.cloned.1.call-done = bf16[4096,512]{1,0:T(8,128)(2,1)} async-done(((bf16[256,512]{1,0:T(8,128)(2,1)}), bf16[4096,512]{1,0:T(8,128)(2,1)}) %all-gather.3.cloned.1.call-update) | async-done | bytes 4194320 | tf_op jit(solution)/shard_map/all_gather | solution.py:132
  149.1 6.8 %fusion.4 = f32[512,512]{0,1:T(8,128)} fusion(bf16[4096,512]{1,0:T(8,128)(2,1)} %all-gather.3.cloned.1.call-done, bf16[1,512,4096]{2,1,0:T(8,128)(2,1)} %all-gather.5.cloned.1.call-done), kind=kOutput, calls=%fused_computation.8 | convolution fusion | flops 2147483648 | bytes 9437184 | tf_op jit(solution)/shard_map/dot_general | solution.py:130
  155.9 1.9 reshape.182
  158.2 1.4 multiply_convert_fusion.2
  159.6 1.3 copy.215
  160.9 6.6 %fusion = bf16[4096,512]{0,1:T(8,128)(2,1)} fusion(bf16[1,512,4096]{2,1,0:T(8,128)(2,1)} %all-gather.5.cloned.1.call-done, bf16[64,8,4,128]{3,2,1,0:T(4,128)(2,1)S(1)} %bitcast.110), kind=kOutput, calls=%fused_computation.1 | convolution fusion | flops 2149580800 | bytes 8912896 | tf_op jit(solution)/shard_map/td,th->dh/dot_general | solution.py:138
  168.5 0.8 copy.219
  170.4 0.8 copy.214
  171.2 0.8 copy.217
  172.1 1.3 collective-permute-start.23
  173.4 1.3 collective-permute-start.21
  174.7 2.9 collective-permute-done.23
  177.5 5.2 %collective-permute-done.21 = f32[4]{0:T(128)S(1)} collective-permute-done((f32[4]{0:T(128)S(1)}, f32[4]{0:T(128)S(1)}, u32[]{:S(2)}, u32[]{:S(2)}) %collective-permute-start.21) | collective-permute-done | bytes 48 | tf_op jit(solution)/shard_map/ppermute | solution.py:49
  183.2 1.4 collective-permute-start.18
  184.6 1.3 collective-permute-start.16
  185.9 1.3 collective-permute-start.14
  188.0 1.5 convolution_bitcast_fusion.4
  189.4 1.5 convolution_bitcast_fusion.5
  191.4 20.1 %collective-permute-done.18 = f32[4,128,128]{2,1,0:T(8,128)S(1)} collective-permute-done((f32[4,128,128]{2,1,0:T(8,128)S(1)}, f32[4,128,128]{2,1,0:T(8,128)S(1)}, u32[]{:S(2)}, u32[]{:S(2)}) %collective-permute-start.18) | collective-permute-done | bytes 262176 | tf_op jit(solution)/shard_map/ppermute | solution.py:49
  211.5 0.9 multiply_add_fusion.3
  212.4 1.3 collective-permute-start.24
  213.6 1.3 collective-permute-start.22
  214.9 1.5 collective-permute-start.20
  217.1 1.0 reshape.176
  218.1 64.2 %reduce-scatter.5.cloned.1.call-done = bf16[256,512]{0,1:T(8,128)(2,1)} async-done(((bf16[4096,512]{0,1:T(8,128)(2,1)}), bf16[256,512]{0,1:T(8,128)(2,1)}) %reduce-scatter.5.cloned.1.call-update) | async-done | bytes 262160 | tf_op jit(solution)/shard_map/reduce_scatter | solution.py:137
  282.3 1.9 copy.237
  284.3 1.2 multiply_add_fusion.2
  285.6 1.7 fusion.17
  287.7 1.0 reshape.178
  289.5 1.0 reshape.177
  290.5 18.7 %reduce-scatter.7.cloned.1.call-done = f32[64,512]{1,0:T(8,128)} async-done(((f32[256,512]{1,0:T(8,128)}), f32[64,512]{1,0:T(8,128)}) %reduce-scatter.7.cloned.1.call-update) | async-done | bytes 131088
  309.2 1.0 copy.238
  310.5 0.8 copy.222
  311.3 0.8 copy.221
  312.1 0.8 copy.220
  (138 shorter events, 11.4 us)
Async XLA Ops:
  7.2 13.6 %copy-start.27 = (f32[1,512,4]{1,2,0:T(4,128)S(1)}, f32[1,512,4]{1,2,0:T(4,128)}, u32[]{:S(2)}) copy-start(f32[1,512,4]{1,2,0:T(4,128)} %param.15) | copy-start | bytes 24580
  7.2 19.5 %copy-start.19 = (bf16[1,512,512]{2,1,0:T(8,128)(2,1)S(1)}, bf16[1,512,512]{2,1,0:T(8,128)(2,1)}, u32[]{:S(2)}) copy-start(bf16[1,512,512]{2,1,0:T(8,128)(2,1)} %param.12) | copy-start | bytes 1572868
  7.2 19.6 %copy-start.20 = (bf16[1,512,512]{2,1,0:T(8,128)(2,1)S(1)}, bf16[1,512,512]{2,1,0:T(8,128)(2,1)}, u32[]{:S(2)}) copy-start(bf16[1,512,512]{2,1,0:T(8,128)(2,1)} %param.13) | copy-start | bytes 1572868
  7.2 114.2 %all-gather.5.cloned.1.call-start = ((), (), s32[]{:S(2)}) async-start(), calls=%async_computation.3 | async-start | bytes 5242880 | tf_op jit(solution)/shard_map/all_gather | solution.py:127
  7.9 141.2 %all-gather.3.cloned.1.call-start = ((), (), s32[]{:S(2)}) async-start(), calls=%async_computation.2 | async-start | bytes 4456448 | tf_op jit(solution)/shard_map/all_gather | solution.py:132
  8.9 5.6 %collective-permute-start.11 = (bf16[64,512]{1,0:T(8,128)(2,1)S(1)}, bf16[64,512]{1,0:T(8,128)(2,1)S(1)}, u32[]{:S(2)}, u32[]{:S(2)}) collective-permute-start(bf16[64,512]{1,0:T(8,128)(2,1)S(1)} %get-tuple-element.50), channel_id=1, source_target_pairs={{0,4},{4,8},{8,12},{12,0},{1,5},{5,9},{9,13},{13,1},{2,6},{6,10},{... | collective-permute-start | bytes 196616 | tf_op jit(solution)/shard_map/ppermute | solution.py:32
  10.6 4.3 %collective-permute-start.12 = (bf16[64,512]{1,0:T(8,128)(2,1)S(1)}, bf16[64,512]{1,0:T(8,128)(2,1)S(1)}, u32[]{:S(2)}, u32[]{:S(2)}) collective-permute-start(bf16[64,512]{1,0:T(8,128)(2,1)S(1)} %get-tuple-element.50), channel_id=1, source_target_pairs={{0,12},{4,0},{8,4},{12,8},{1,13},{5,1},{9,5},{13,9},{2,14},{6,2},{... | collective-permute-start | bytes 196616 | tf_op jit(solution)/shard_map/ppermute | solution.py:35
  14.5 5.5 %collective-permute-start.13 = (bf16[64,512]{1,0:T(8,128)(2,1)S(1)}, bf16[64,512]{1,0:T(8,128)(2,1)S(1)}, u32[]{:S(2)}, u32[]{:S(2)}) collective-permute-start(bf16[64,512]{1,0:T(8,128)(2,1)S(1)} %collective-permute-done.11), channel_id=1, source_target_pairs={{0,4},{4,8},{8,12},{12,0},{1,5},{5,9},{9,13},{13,1},{2,6},{6,10},{... | collective-permute-start | bytes 196616 | tf_op jit(solution)/shard_map/ppermute | solution.py:32
  20.0 0.7 copy-start.13
  20.7 261.6 %reduce-scatter.5.cloned.1.call-start = ((), (), s32[]{:S(2)}) async-start(), calls=%async_computation.4 | async-start | bytes 4456448 | tf_op jit(solution)/shard_map/reduce_scatter | solution.py:137
  23.9 24.2 %copy-start.21 = (bf16[1,512,512]{2,1,0:T(8,128)(2,1)S(1)}, bf16[1,512,512]{2,1,0:T(8,128)(2,1)}, u32[]{:S(2)}) copy-start(bf16[1,512,512]{2,1,0:T(8,128)(2,1)} %param.11) | copy-start | bytes 1572868
  24.0 27.0 %collective-permute-start.19 = (f32[4]{0:T(128)S(1)}, f32[4]{0:T(128)S(1)}, u32[]{:S(2)}, u32[]{:S(2)}) collective-permute-start(f32[4]{0:T(128)S(1)} %get-tuple-element.40), channel_id=1, source_target_pairs={{48,0},{64,16},{80,32},{96,48},{112,64},{128,80},{144,96},{160,112... | collective-permute-start | bytes 56 | tf_op jit(solution)/shard_map/ppermute | solution.py:49
  25.4 26.9 %collective-permute-start.17 = (f32[4]{0:T(128)S(1)}, f32[4]{0:T(128)S(1)}, u32[]{:S(2)}, u32[]{:S(2)}) collective-permute-start(f32[4]{0:T(128)S(1)} %get-tuple-element.40), channel_id=1, source_target_pairs={{32,0},{48,16},{64,32},{80,48},{96,64},{112,80},{128,96},{144,112}... | collective-permute-start | bytes 56 | tf_op jit(solution)/shard_map/ppermute | solution.py:49
  26.8 21.7 %copy-start.5 = (bf16[2,256,4,128]{3,2,1,0:T(4,128)(2,1)}, bf16[2,256,4,128]{3,2,1,0:T(4,128)(2,1)S(1)}, u32[]{:S(2)}) copy-start(bf16[2,256,4,128]{3,2,1,0:T(4,128)(2,1)S(1)} %reshape.170) | copy-start | bytes 1572868
  27.0 22.4 %copy-start.3 = (bf16[2,256,4,128]{3,2,1,0:T(4,128)(2,1)}, bf16[2,256,4,128]{3,2,1,0:T(4,128)(2,1)S(1)}, u32[]{:S(2)}) copy-start(bf16[2,256,4,128]{3,2,1,0:T(4,128)(2,1)S(1)} %reshape.174) | copy-start | bytes 1572868
  29.1 45.9 %collective-permute-start.4 = (f32[4,128,128]{2,1,0:T(8,128)}, f32[4,128,128]{2,1,0:T(8,128)}, u32[]{:S(2)}, u32[]{:S(2)}) collective-permute-start(f32[4,128,128]{2,1,0:T(8,128)} %fusion.33), channel_id=1, source_target_pairs={{0,48},{16,64},{32,80},{48,96},{64,112},{80,128},{96,144},{112,160... | collective-permute-start | bytes 786440 | tf_op jit(solution)/shard_map/ppermute | solution.py:49
  37.5 37.4 %collective-permute-start.2 = (f32[4,128,128]{2,1,0:T(8,128)}, f32[4,128,128]{2,1,0:T(8,128)}, u32[]{:S(2)}, u32[]{:S(2)}) collective-permute-start(f32[4,128,128]{2,1,0:T(8,128)} %fusion.33), channel_id=1, source_target_pairs={{0,32},{16,48},{32,64},{48,80},{64,96},{80,112},{96,128},{112,144}... | collective-permute-start | bytes 786440 | tf_op jit(solution)/shard_map/ppermute | solution.py:49
  44.3 30.6 %collective-permute-start = (f32[4,128,128]{2,1,0:T(8,128)}, f32[4,128,128]{2,1,0:T(8,128)}, u32[]{:S(2)}, u32[]{:S(2)}) collective-permute-start(f32[4,128,128]{2,1,0:T(8,128)} %fusion.33), channel_id=1, source_target_pairs={{0,16},{16,32},{32,48},{48,64},{64,80},{80,96},{96,112},{112,128},... | collective-permute-start | bytes 786440 | tf_op jit(solution)/shard_map/ppermute | solution.py:49
  48.6 71.0 %copy-start = (bf16[2,256,4,128]{1,3,2,0:T(8,128)(2,1)}, bf16[2,256,4,128]{1,3,2,0:T(8,128)(2,1)S(1)}, u32[]{:S(2)}) copy-start(bf16[2,256,4,128]{1,3,2,0:T(8,128)(2,1)S(1)} %copy.204) | copy-start | bytes 1572868
  48.6 2.2 copy-start.22
  49.3 26.6 %copy-start.8 = (bf16[2,4,256,256]{3,2,1,0:T(8,128)(2,1)}, bf16[2,4,256,256]{3,2,1,0:T(8,128)(2,1)S(1)}, u32[]{:S(2)}) copy-start(bf16[2,4,256,256]{3,2,1,0:T(8,128)(2,1)S(1)} %multiply_convert_fusion.1) | copy-start | bytes 3145732
  49.4 49.1 %copy-start.17 = (bf16[1,512,512]{2,1,0:T(8,128)(2,1)S(1)}, bf16[1,512,512]{2,1,0:T(8,128)(2,1)}, u32[]{:S(2)}) copy-start(bf16[1,512,512]{2,1,0:T(8,128)(2,1)} %param.14) | copy-start | bytes 1572868
  51.0 8.5 %collective-permute-start.15 = (f32[4]{0:T(128)S(1)}, f32[4]{0:T(128)S(1)}, u32[]{:S(2)}, u32[]{:S(2)}) collective-permute-start(f32[4]{0:T(128)S(1)} %get-tuple-element.40), channel_id=1, source_target_pairs={{16,0},{32,16},{48,32},{64,48},{80,64},{96,80},{112,96},{128,112},... | collective-permute-start | bytes 56 | tf_op jit(solution)/shard_map/ppermute | solution.py:49
  52.3 17.7 %collective-permute-start.5 = (f32[4]{0:T(128)S(1)}, f32[4]{0:T(128)S(1)}, u32[]{:S(2)}, u32[]{:S(2)}) collective-permute-start(f32[4]{0:T(128)S(1)} %get-tuple-element.40), channel_id=1, source_target_pairs={{0,48},{16,64},{32,80},{48,96},{64,112},{80,128},{96,144},{112,160... | collective-permute-start | bytes 56 | tf_op jit(solution)/shard_map/ppermute | solution.py:49
  59.4 14.2 %collective-permute-start.3 = (f32[4]{0:T(128)S(1)}, f32[4]{0:T(128)S(1)}, u32[]{:S(2)}, u32[]{:S(2)}) collective-permute-start(f32[4]{0:T(128)S(1)} %get-tuple-element.40), channel_id=1, source_target_pairs={{0,32},{16,48},{32,64},{48,80},{64,96},{80,112},{96,128},{112,144}... | collective-permute-start | bytes 56 | tf_op jit(solution)/shard_map/ppermute | solution.py:49
  70.0 4.9 %collective-permute-start.1 = (f32[4]{0:T(128)S(1)}, f32[4]{0:T(128)S(1)}, u32[]{:S(2)}, u32[]{:S(2)}) collective-permute-start(f32[4]{0:T(128)S(1)} %get-tuple-element.40), channel_id=1, source_target_pairs={{0,16},{16,32},{32,48},{48,64},{64,80},{80,96},{96,112},{112,128},... | collective-permute-start | bytes 56 | tf_op jit(solution)/shard_map/ppermute | solution.py:49
  75.9 43.5 %copy-start.12 = (f32[4,128,128]{2,1,0:T(8,128)S(1)}, f32[4,128,128]{2,1,0:T(8,128)}, u32[]{:S(2)}) copy-start(f32[4,128,128]{2,1,0:T(8,128)} %get-tuple-element.58) | copy-start | bytes 786436
  75.9 42.8 %collective-permute-start.10 = (f32[4,128,128]{2,1,0:T(8,128)}, f32[4,128,128]{2,1,0:T(8,128)S(1)}, u32[]{:S(2)}, u32[]{:S(2)}) collective-permute-start(f32[4,128,128]{2,1,0:T(8,128)} %get-tuple-element.57), channel_id=1, source_target_pairs={{0,192},{16,208},{32,224},{48,240},{1,193},{17,209},{33,225},{49,2... | collective-permute-start | bytes 786440 | tf_op jit(solution)/shard_map/ppermute | solution.py:49
  93.2 25.5 %collective-permute-start.8 = (f32[4,128,128]{2,1,0:T(8,128)}, f32[4,128,128]{2,1,0:T(8,128)}, u32[]{:S(2)}, u32[]{:S(2)}) collective-permute-start(f32[4,128,128]{2,1,0:T(8,128)} %get-tuple-element.57), channel_id=1, source_target_pairs={{0,128},{16,144},{32,160},{48,176},{64,192},{80,208},{96,224},{112... | collective-permute-start | bytes 786440 | tf_op jit(solution)/shard_map/ppermute | solution.py:49
  95.2 23.5 %collective-permute-start.6 = (f32[4,128,128]{2,1,0:T(8,128)}, f32[4,128,128]{2,1,0:T(8,128)}, u32[]{:S(2)}, u32[]{:S(2)}) collective-permute-start(f32[4,128,128]{2,1,0:T(8,128)} %get-tuple-element.57), channel_id=1, source_target_pairs={{0,64},{16,80},{32,96},{48,112},{64,128},{80,144},{96,160},{112,17... | collective-permute-start | bytes 786440 | tf_op jit(solution)/shard_map/ppermute | solution.py:49
  99.1 9.5 %collective-permute-start.9 = (f32[4]{0:T(128)S(1)}, f32[4]{0:T(128)S(1)}, u32[]{:S(2)}, u32[]{:S(2)}) collective-permute-start(f32[4]{0:T(128)S(1)} %get-tuple-element.66), channel_id=1, source_target_pairs={{0,128},{16,144},{32,160},{48,176},{64,192},{80,208},{96,224},{112... | collective-permute-start | bytes 56 | tf_op jit(solution)/shard_map/ppermute | solution.py:49
  100.4 18.2 %collective-permute-start.7 = (f32[4]{0:T(128)S(1)}, f32[4]{0:T(128)S(1)}, u32[]{:S(2)}, u32[]{:S(2)}) collective-permute-start(f32[4]{0:T(128)S(1)} %get-tuple-element.66), channel_id=1, source_target_pairs={{0,64},{16,80},{32,96},{48,112},{64,128},{80,144},{96,160},{112,17... | collective-permute-start | bytes 56 | tf_op jit(solution)/shard_map/ppermute | solution.py:49
  118.7 0.7 copy-start.24
  119.5 29.6 %copy-start.10 = (f32[4,128,128]{2,1,0:T(8,128)}, f32[4,128,128]{2,1,0:T(8,128)S(1)}, u32[]{:S(2)}) copy-start(f32[4,128,128]{2,1,0:T(8,128)S(1)} %multiply_add_fusion.5) | copy-start | bytes 786436
  167.5 0.9 copy-start.18
  167.6 2.5 copy-start.28
  167.6 2.8 copy-start.25
  167.6 3.7 %copy-start.26 = (f32[64,512]{1,0:T(8,128)S(1)}, f32[64,512]{1,0:T(8,128)}, u32[]{:S(2)}) copy-start(f32[64,512]{1,0:T(8,128)} %param.19) | copy-start | bytes 393220
  167.6 15.2 %copy-start.1 = (bf16[2,256,4,128]{1,3,2,0:T(8,128)(2,1)S(1)}, bf16[2,256,4,128]{1,3,2,0:T(8,128)(2,1)}, u32[]{:S(2)}) copy-start(bf16[2,256,4,128]{1,3,2,0:T(8,128)(2,1)} %copy-done) | copy-start | bytes 1572868
  167.6 15.2 %copy-start.2 = (bf16[2,256,4,128]{1,3,2,0:T(8,128)(2,1)S(1)}, bf16[2,256,4,128]{1,3,2,0:T(8,128)(2,1)}, u32[]{:S(2)}) copy-start(bf16[2,256,4,128]{1,3,2,0:T(8,128)(2,1)} %get-tuple-element.60) | copy-start | bytes 1572868
  167.6 19.6 %copy-start.4 = (bf16[2,256,4,128]{3,2,1,0:T(4,128)(2,1)S(1)}, bf16[2,256,4,128]{3,2,1,0:T(4,128)(2,1)}, u32[]{:S(2)}) copy-start(bf16[2,256,4,128]{3,2,1,0:T(4,128)(2,1)} %copy-done.3) | copy-start | bytes 1572868
  167.6 19.6 %copy-start.23 = (f32[256,256]{1,0:T(8,128)S(1)}, f32[256,256]{1,0:T(8,128)}, u32[]{:S(2)}) copy-start(f32[256,256]{1,0:T(8,128)} %copy-done.22) | copy-start | bytes 786436
  167.6 141.6 %reduce-scatter.7.cloned.1.call-start = ((), (), s32[]{:S(2)}) async-start(), calls=%async_computation.5 | async-start | bytes 655360
  172.1 5.5 %collective-permute-start.23 = (f32[4]{0:T(128)S(1)}, f32[4]{0:T(128)S(1)}, u32[]{:S(2)}, u32[]{:S(2)}) collective-permute-start(f32[4]{0:T(128)S(1)} %get-tuple-element.43), channel_id=1, source_target_pairs={{128,0},{144,16},{160,32},{176,48},{192,64},{208,80},{224,96},{240... | collective-permute-start | bytes 56 | tf_op jit(solution)/shard_map/ppermute | solution.py:49
  173.4 9.4 %collective-permute-start.21 = (f32[4]{0:T(128)S(1)}, f32[4]{0:T(128)S(1)}, u32[]{:S(2)}, u32[]{:S(2)}) collective-permute-start(f32[4]{0:T(128)S(1)} %get-tuple-element.43), channel_id=1, source_target_pairs={{64,0},{80,16},{96,32},{112,48},{128,64},{144,80},{160,96},{176,11... | collective-permute-start | bytes 56 | tf_op jit(solution)/shard_map/ppermute | solution.py:49
  183.1 4.9 %copy-start.9 = (bf16[2,4,256,256]{3,2,1,0:T(8,128)(2,1)S(1)}, bf16[2,4,256,256]{3,2,1,0:T(8,128)(2,1)}, u32[]{:S(2)}) copy-start(bf16[2,4,256,256]{3,2,1,0:T(8,128)(2,1)} %copy-done.8) | copy-start | bytes 3145732
  183.2 28.3 %collective-permute-start.18 = (f32[4,128,128]{2,1,0:T(8,128)S(1)}, f32[4,128,128]{2,1,0:T(8,128)S(1)}, u32[]{:S(2)}, u32[]{:S(2)}) collective-permute-start(f32[4,128,128]{2,1,0:T(8,128)S(1)} %fusion.32), channel_id=1, source_target_pairs={{48,0},{64,16},{80,32},{96,48},{112,64},{128,80},{144,96},{160,112... | collective-permute-start | bytes 786440 | tf_op jit(solution)/shard_map/ppermute | solution.py:49
  184.6 26.9 %collective-permute-start.16 = (f32[4,128,128]{2,1,0:T(8,128)S(1)}, f32[4,128,128]{2,1,0:T(8,128)S(1)}, u32[]{:S(2)}, u32[]{:S(2)}) collective-permute-start(f32[4,128,128]{2,1,0:T(8,128)S(1)} %fusion.32), channel_id=1, source_target_pairs={{32,0},{48,16},{64,32},{80,48},{96,64},{112,80},{128,96},{144,112}... | collective-permute-start | bytes 786440 | tf_op jit(solution)/shard_map/ppermute | solution.py:49
  185.9 25.6 %collective-permute-start.14 = (f32[4,128,128]{2,1,0:T(8,128)S(1)}, f32[4,128,128]{2,1,0:T(8,128)S(1)}, u32[]{:S(2)}, u32[]{:S(2)}) collective-permute-start(f32[4,128,128]{2,1,0:T(8,128)S(1)} %fusion.32), channel_id=1, source_target_pairs={{16,0},{32,16},{48,32},{64,48},{80,64},{96,80},{112,96},{128,112},... | collective-permute-start | bytes 786440 | tf_op jit(solution)/shard_map/ppermute | solution.py:49
  188.0 3.0 copy-start.6
  190.9 25.5 %copy-start.11 = (f32[4,128,128]{2,1,0:T(8,128)S(1)}, f32[4,128,128]{2,1,0:T(8,128)}, u32[]{:S(2)}) copy-start(f32[4,128,128]{2,1,0:T(8,128)} %copy-done.10) | copy-start | bytes 786436
  212.4 72.0 %collective-permute-start.24 = (f32[4,128,128]{2,1,0:T(8,128)}, f32[4,128,128]{2,1,0:T(8,128)}, u32[]{:S(2)}, u32[]{:S(2)}) collective-permute-start(f32[4,128,128]{2,1,0:T(8,128)} %get-tuple-element.47), channel_id=1, source_target_pairs={{192,0},{208,16},{224,32},{240,48},{193,1},{209,17},{225,33},{241,... | collective-permute-start | bytes 786440 | tf_op jit(solution)/shard_map/ppermute | solution.py:49
  213.6 70.7 %collective-permute-start.22 = (f32[4,128,128]{2,1,0:T(8,128)}, f32[4,128,128]{2,1,0:T(8,128)}, u32[]{:S(2)}, u32[]{:S(2)}) collective-permute-start(f32[4,128,128]{2,1,0:T(8,128)} %get-tuple-element.47), channel_id=1, source_target_pairs={{128,0},{144,16},{160,32},{176,48},{192,64},{208,80},{224,96},{240... | collective-permute-start | bytes 786440 | tf_op jit(solution)/shard_map/ppermute | solution.py:49
  214.9 69.4 %collective-permute-start.20 = (f32[4,128,128]{2,1,0:T(8,128)}, f32[4,128,128]{2,1,0:T(8,128)}, u32[]{:S(2)}, u32[]{:S(2)}) collective-permute-start(f32[4,128,128]{2,1,0:T(8,128)} %get-tuple-element.47), channel_id=1, source_target_pairs={{64,0},{80,16},{96,32},{112,48},{128,64},{144,80},{160,96},{176,11... | collective-permute-start | bytes 786440 | tf_op jit(solution)/shard_map/ppermute | solution.py:49
  285.6 3.1 copy-start.7
  288.7 21.5 %copy-start.14 = (f32[64,512]{0,1:T(8,128)S(1)}, f32[64,512]{0,1:T(8,128)}, u32[]{:S(2)}) copy-start(f32[64,512]{0,1:T(8,128)} %copy.219) | copy-start | bytes 393220
  288.7 21.5 %copy-start.15 = (f32[64,512]{0,1:T(8,128)S(1)}, f32[64,512]{0,1:T(8,128)}, u32[]{:S(2)}) copy-start(f32[64,512]{0,1:T(8,128)} %copy.214) | copy-start | bytes 393220
  288.7 21.5 %copy-start.16 = (f32[64,512]{0,1:T(8,128)S(1)}, f32[64,512]{0,1:T(8,128)}, u32[]{:S(2)}) copy-start(f32[64,512]{0,1:T(8,128)} %copy.217) | copy-start | bytes 393220
Sparse Core Ops, SparseCore 0:
  9.8 44.8 all-gather.4
  56.5 92.5 all-gather.2
  167.7 114.5 reduce-scatter.4
  284.7 24.4 reduce-scatter.6
